TPU v7x, 32 devices: a whole 2x2x4 slice. The times are simulated.
32 devices in a mesh: groups: 2 (over y), ctx: 4 (over z), sub: 2 (over x), head: 2 (over core).
Axes of the slice: x: 2, y: 2, z: 4, core: 2. Of those that a mesh axis runs over, the one named last changes fastest.
Arguments:
- queries: bfloat16 [32, 10240, 128], P(('sub', 'head'), ('groups', 'ctx')), parts along dimension 1, may hold values from -6 to 6
- keys: bfloat16 [32, 10240, 128], P(('sub', 'head'), ('groups', 'ctx')), parts along dimension 1, may hold values from -6 to 6
- values: bfloat16 [32, 10240, 128], P(('sub', 'head'), ('groups', 'ctx')), parts along dimension 1, may hold values from -90 to 90
- out_grad: bfloat16 [32, 10240, 128], P(('sub', 'head'), ('groups', 'ctx')), parts along dimension 1, may hold values from -6 to 6
- norm_gain: float32 [32, 128], P(('sub', 'head')), may hold values from 0.25 to 1.75
- doc_ids: int32 [40], P(('groups', 'ctx')), parts along dimension 0, may hold values from 0 to 3, never falling along the last dimension, each value on 1 to 10 neighbouring positions
Outputs:
- grad_queries: bfloat16 [32, 10240, 128], P(('sub', 'head'), ('groups', 'ctx')), parts along dimension 1
- grad_keys: bfloat16 [32, 10240, 128], P(('sub', 'head'), ('groups', 'ctx')), parts along dimension 1
- grad_values: bfloat16 [32, 10240, 128], P(('sub', 'head'), ('groups', 'ctx')), parts along dimension 1
There are 2 independent parts, one for each index of `groups`. A program takes and returns all parts, laid end to end along the dimension named above; an argument that names none is the same for every part. Nothing has to cross between parts.
Inputs may be any that keep to these rules, and one draw needn't show every extreme that they name: `doc_ids`: never falls; each of its 4 values labels 1 to 10 consecutive blocks, one value exactly 10.
All inputs are finite; a program needn't handle non-finite values.
Results may differ from a plain program's by a relative error of at most 0.0058.
Values sent between devices are 32-bit elements; how exact they have to be, the bound alone decides.
No kernel may reach another device: no remote copies, remote signals or barrier semaphores. Data moves between devices by JAX's collectives and lax.ppermute only.
A program may use at most 128 MiB of HBM per device.

v0:
```python
import jax
import jax.numpy as jnp
from jax import lax
from jax.sharding import PartitionSpec as P


def segmented_scan(doc, state, axis, reverse):
    peers = lax.axis_size(axis)
    index = lax.axis_index(axis)
    none_doc = jnp.float32(-1.0)

    def shift(value, step):
        if reverse:
            pairs = [(j, j - step) for j in range(step, peers)]
        else:
            pairs = [(j, j + step) for j in range(peers - step)]
        return lax.ppermute(value, axis, pairs)

    def combine(near_doc, near_state, far_doc, far_state):
        joined = (near_doc == far_doc).astype(jnp.float32)
        return (near_doc, near_state + joined * far_state)

    if peers == 1:
        return (none_doc, jnp.zeros_like(state))
    got_doc, got_state = shift((doc, state), 1)
    valid = index >= 1 if not reverse else index <= peers - 2
    ex_doc = jnp.where(valid, got_doc, none_doc)
    ex_state = jnp.where(valid, got_state, 0.0)
    in_doc, in_state = combine(doc, state, ex_doc, ex_state)
    covered = 1
    while covered < peers - 1:
        step = covered + 1
        got_doc, got_state = shift((in_doc, in_state), step)
        valid = index >= step if not reverse else index <= peers - 1 - step
        got_doc = jnp.where(valid, got_doc, none_doc)
        got_state = jnp.where(valid, got_state, 0.0)
        ex_doc, ex_state = combine(ex_doc, ex_state, got_doc, got_state)
        covered = covered + step
        if covered < peers - 1:
            in_doc, in_state = combine(in_doc, in_state, got_doc, got_state)
    return (ex_doc, ex_state)


def on_device(queries, keys, values, out_grad, norm_gain, doc_ids):
    head_count, tok_count, head_width = queries.shape
    block_count = doc_ids.shape[0]
    block_len = tok_count // block_count
    block_shape = (head_count, block_count, block_len, head_width)
    highest_precision = lax.Precision.HIGHEST
    query_blocks = queries.reshape(block_shape)
    key_blocks = keys.reshape(block_shape)
    value_blocks = values.reshape(block_shape)
    row_ids = lax.broadcasted_iota(jnp.int32, (block_len, block_len), 0)
    col_ids = lax.broadcasted_iota(jnp.int32, (block_len, block_len), 1)
    causal = row_ids >= col_ids
    doc_values = doc_ids.astype(jnp.float32)
    block_pos = jnp.arange(block_count, dtype=jnp.int32)
    same_doc = doc_values[:, None] == doc_values[None, :]
    earlier_mask = (same_doc & (block_pos[None, :] < block_pos[:, None])).astype(jnp.float32)
    later_mask = (same_doc & (block_pos[None, :] > block_pos[:, None])).astype(jnp.float32)
    key_value_block = jnp.einsum(
        "hnid,hnie->hnde", key_blocks, value_blocks, preferred_element_type=jnp.float32
    )
    last_match = (doc_values == doc_values[-1]).astype(jnp.float32)
    device_kv = jnp.einsum("c,hcde->hde", last_match, key_value_block, precision=highest_precision)
    prior_doc, prior_state = segmented_scan(doc_values[-1], device_kv, "ctx", False)
    scores = jnp.einsum(
        "hnid,hnjd->hnij", query_blocks, key_blocks, preferred_element_type=jnp.float32
    )
    block_probs = jnp.where(causal, scores, 0.0).astype(jnp.bfloat16)
    intra_part = jnp.einsum(
        "hnij,hnjd->hnid", block_probs, value_blocks, preferred_element_type=jnp.float32
    )
    local_prefix = jnp.einsum(
        "bc,hcde->hbde", earlier_mask, key_value_block, precision=highest_precision
    )
    prior_match = (doc_values == prior_doc).astype(jnp.float32)
    entering = prior_match[None, :, None, None] * prior_state[:, None, :, :]
    preceding_states = (local_prefix + entering).astype(jnp.bfloat16)
    cross_block_part = jnp.einsum(
        "hnid,hnde->hnie", query_blocks, preceding_states, preferred_element_type=jnp.float32
    )
    raw_attn = (intra_part + cross_block_part).reshape(head_count, tok_count, head_width)
    feature_count = head_count * head_width * lax.axis_size(("sub", "head"))
    scaled = norm_gain[:, None, :] * out_grad.astype(jnp.float32)
    local_sums = jnp.stack(
        [jnp.sum(raw_attn * raw_attn, axis=(0, 2)), jnp.sum(scaled * raw_attn, axis=(0, 2))]
    )
    total_sums = lax.psum(local_sums, ("sub", "head"))
    root_mean = jnp.sqrt(total_sums[0] / feature_count + 1e-06)
    inner_mean = total_sums[1] / feature_count
    factor = inner_mean / (root_mean * root_mean)
    d_attn = ((scaled - raw_attn * factor[None, :, None]) / root_mean[None, :, None]).astype(
        jnp.bfloat16
    )
    output_grad_blocks = d_attn.reshape(block_shape)
    query_grad_block = jnp.einsum(
        "hnid,hnie->hnde", query_blocks, output_grad_blocks, preferred_element_type=jnp.float32
    )
    first_match = (doc_values == doc_values[0]).astype(jnp.float32)
    device_qd = jnp.einsum(
        "c,hcde->hde", first_match, query_grad_block, precision=highest_precision
    )
    next_doc, next_state = segmented_scan(doc_values[0], device_qd, "ctx", True)
    grad_scores = jnp.einsum(
        "hnid,hnjd->hnij", output_grad_blocks, value_blocks, preferred_element_type=jnp.float32
    )
    grad_probs = jnp.where(causal, grad_scores, 0.0).astype(jnp.bfloat16)
    query_gradient = jnp.einsum(
        "hnij,hnjd->hnid", grad_probs, key_blocks, preferred_element_type=jnp.float32
    )
    key_gradient = jnp.einsum(
        "hnij,hnid->hnjd", grad_probs, query_blocks, preferred_element_type=jnp.float32
    )
    value_gradient = jnp.einsum(
        "hnij,hnid->hnjd", block_probs, output_grad_blocks, preferred_element_type=jnp.float32
    )
    local_suffix = jnp.einsum(
        "bc,hcde->hbde", later_mask, query_grad_block, precision=highest_precision
    )
    next_match = (doc_values == next_doc).astype(jnp.float32)
    leaving = next_match[None, :, None, None] * next_state[:, None, :, :]
    following_states = (local_suffix + leaving).astype(jnp.bfloat16)
    query_gradient = query_gradient + jnp.einsum(
        "hnie,hnde->hnid", output_grad_blocks, preceding_states, preferred_element_type=jnp.float32
    )
    key_gradient = key_gradient + jnp.einsum(
        "hnie,hnde->hnid", value_blocks, following_states, preferred_element_type=jnp.float32
    )
    value_gradient = value_gradient + jnp.einsum(
        "hnid,hnde->hnie", key_blocks, following_states, preferred_element_type=jnp.float32
    )
    out_shape = (head_count, tok_count, head_width)
    return (
        query_gradient.reshape(out_shape).astype(jnp.bfloat16),
        key_gradient.reshape(out_shape).astype(jnp.bfloat16),
        value_gradient.reshape(out_shape).astype(jnp.bfloat16),
    )


def solution(mesh):
    return jax.shard_map(
        on_device,
        mesh=mesh,
        in_specs=(
            P(("sub", "head"), ("groups", "ctx"), None),
            P(("sub", "head"), ("groups", "ctx"), None),
            P(("sub", "head"), ("groups", "ctx"), None),
            P(("sub", "head"), ("groups", "ctx"), None),
            P(("sub", "head"), None),
            P(("groups", "ctx")),
        ),
        out_specs=(
            P(("sub", "head"), ("groups", "ctx"), None),
            P(("sub", "head"), ("groups", "ctx"), None),
            P(("sub", "head"), ("groups", "ctx"), None),
        ),
        check_vma=False,
    )
```

profile of v0, /device:TPU:0, one launch (start us, length us, event | category | flops | bytes accessed | tf_op | source)
XLA Modules:
  0.0 159.0 jit_solution(8993034932632156992)
XLA Ops:
  0.6 0.0 copy-start
  0.6 0.8 convert_element_type.63
  1.5 0.6 fusion.34
  2.0 1.3 collective-permute-start.6
  3.3 1.3 collective-permute-start.4
  4.6 7.6 %collective-permute-start.2 = (f32[]{:T(128)}, f32[]{:T(128)}, u32[]{:S(2)}, u32[]{:S(2)}) collective-permute-start(f32[]{:T(128)} %bitcast.7), channel_id=1, source_target_pairs={{0,8},{4,12},{1,9},{5,13},{2,10},{6,14},{3,11},{7,15},{16,24},{20,... | collective-permute-start | bytes 20 | tf_op jit(solution)/shard_map/ppermute | solution.py:17
  12.2 5.0 %collective-permute-start = (f32[]{:T(128)}, f32[]{:T(128)}, u32[]{:S(2)}, u32[]{:S(2)}) collective-permute-start(f32[]{:T(128)} %bitcast.7), channel_id=1, source_target_pairs={{0,4},{4,8},{8,12},{1,5},{5,9},{9,13},{2,6},{6,10},{10,14},{3,7},{... | collective-permute-start | bytes 20 | tf_op jit(solution)/shard_map/ppermute | solution.py:17
  17.2 3.4 %fusion.36 = f32[8,5,128,128]{3,2,1,0:T(8,128)S(1)} fusion(bf16[8,5,256,128]{3,2,1,0:T(8,128)(2,1)} %bitcast.105, bf16[8,5,256,128]{3,2,1,0:T(8,128)(2,1)} %bitcast.109), kind=kOutput, calls=%fused_computation.62 | convolution fusion | flops 335544320 | bytes 7864320 | tf_op jit(solution)/shard_map/hnid,hnie->hnde/dot_general | solution.py:61
  20.6 0.0 copy-start.2
  20.6 1.5 copy-done.2
  22.1 4.9 %fusion.6 = f32[1,8,128,128]{3,0,2,1:T(1,128)} fusion(f32[8,5,128,128]{3,2,1,0:T(8,128)S(1)} %fusion.36, f32[]{:T(128)} %bitcast.7, s32[5]{0:T(128)S(1)} %copy-done.16), kind=kOutput, calls=%fused_computation.16 | convolution fusion | flops 7864330 | bytes 3145752 | tf_op jit(solution)/shard_map/c,hcde->hde/dot_general | solution.py:65
  27.0 1.4 collective-permute-start.1
  28.5 0.0 copy-start.9
  28.5 3.4 %select_convert_fusion.1 = bf16[8,5,256,256]{3,2,1,0:T(8,128)(2,1)S(1)} fusion(pred[256,256]{1,0:T(8,128)(4,1)S(1)} %iota_compare_fusion, bf16[8,5,256,128]{3,2,1,0:T(8,128)(2,1)S(1)} %bitcast.95, bf16[8,5,256,128]{3,2,1,0:T(8,128)(2,1)} %bitcast.106), kind=kOutput, calls=%fused_computation.1 | convolution fusion | flops 676331520 | bytes 10551296 | tf_op jit(solution)/shard_map/hnid,hnjd->hnij/dot_general | solution.py:67
  31.9 4.0 %fusion.35 = f32[8,5,256,128]{3,2,1,0:T(8,128)} fusion(bf16[8,5,256,256]{3,2,1,0:T(8,128)(2,1)S(1)} %select_convert_fusion.1, bf16[8,5,256,128]{3,2,1,0:T(8,128)(2,1)S(1)} %bitcast.110), kind=kOutput, calls=%fused_computation.61 | convolution fusion | flops 671088640 | bytes 13107200 | tf_op jit(solution)/shard_map/hnij,hnjd->hnid/dot_general | solution.py:71
  35.9 0.0 collective-permute-done
  37.2 2.1 %collective-permute-done.1 = f32[8,128,128]{2,1,0:T(8,128)S(1)} collective-permute-done((f32[8,128,128]{2,1,0:T(8,128)}, f32[8,128,128]{2,1,0:T(8,128)S(1)}, u32[]{:S(2)}, u32[]{:S(2)}) %collective-permute-start.1) | collective-permute-done | bytes 524320 | tf_op jit(solution)/shard_map/ppermute | solution.py:17
  39.3 1.9 %multiply_add_fusion.3 = f32[8,128,128]{2,1,0:T(8,128)} fusion(f32[8,128,128]{2,1,0:T(8,128)} %bitcast.11, f32[8,128,128]{2,1,0:T(8,128)S(1)} %collective-permute-done.1, f32[]{:T(128)S(6)} %convert_element_type.66, pred[]{:T(512)S(6)} %ge.12), kind=kLoop, calls=%fused_computation.28 | loop fusion | flops 393216 | bytes 1572869 | tf_op jit(solution)/shard_map/add | solution.py:21
  41.2 4.8 %collective-permute-start.3 = (f32[8,128,128]{2,1,0:T(8,128)}, f32[8,128,128]{2,1,0:T(8,128)}, u32[]{:S(2)}, u32[]{:S(2)}) collective-permute-start(f32[8,128,128]{2,1,0:T(8,128)} %multiply_add_fusion.3), channel_id=1, source_target_pairs={{0,8},{4,12},{1,9},{5,13},{2,10},{6,14},{3,11},{7,15},{16,24},{20,... | collective-permute-start | bytes 1572872 | tf_op jit(solution)/shard_map/ppermute | solution.py:17
  46.0 7.2 %fusion.8 = f32[8,128,128,5]{2,3,1,0:T(8,128)} fusion(f32[8,5,128,128]{3,2,1,0:T(8,128)} %copy-done.2, f32[5]{0:T(128)S(1)} %convert_element_type.63), kind=kOutput, calls=%fused_computation.18 | convolution fusion | flops 39321676 | bytes 5242900 | tf_op jit(solution)/shard_map/bc,hcde->hbde/dot_general | solution.py:74
  53.2 0.0 collective-permute-done.4
  54.4 0.0 collective-permute-done.6
  55.1 0.0 collective-permute-done.2
  55.7 0.0 collective-permute-done.3
  55.7 0.1 multiply_add_fusion.2
  55.8 3.0 %fusion.11 = bf16[8,5,128,128]{3,2,1,0:T(8,128)(2,1)S(1)} fusion(f32[8,128,128,5]{2,3,1,0:T(8,128)} %fusion.8, f32[8,128,128]{2,1,0:T(8,128)S(1)} %multiply_add_fusion.2, f32[5]{0:T(128)S(1)} %get-tuple-element.6), kind=kLoop, calls=%fused_computation.23 | loop fusion | flops 1966080 | bytes 4456468 | tf_op jit(solution)/shard_map/convert_element_type | solution.py:79
  58.8 0.8 copy-done.7
  59.5 1.2 multiply_reduce_fusion
  60.7 0.0 copy-start.1
  60.8 1.1 copy-done.14
  61.9 0.8 fusion.2
  62.6 0.4 copy-done.1
  63.1 10.3 %psum.7 = f32[2,1280]{1,0:T(2,128)S(1)} all-reduce(f32[2,1280]{1,0:T(2,128)S(1)} %pad_maximum_fusion), channel_id=1, replica_groups=mesh['groups'=2,'ctx'=4,'sub'=2,'head'=2] {'sub','head'}, use_global_device_ids=true, to_apply=%region_2.3 | all-reduce | flops 2560 | bytes 20480 | tf_op jit(solution)/shard_map/psum | solution.py:89
  73.5 4.0 %fusion.5 = bf16[8,1280,128]{2,1,0:T(8,128)(2,1)S(1)} fusion(f32[8,5,256,128]{3,2,1,0:T(8,128)} %copy-done.1, bf16[8,1280,128]{2,1,0:T(8,128)(2,1)} %param.9, f32[1280]{0:T(1024)S(1)} %get-tuple-element.4, f32[1280]{0:T(1024)S(1)} %multiply_divide_fusion, f32[8,128]{1,0:T(8,128)S(1)} %copy-done.15), kind=kLoop, calls=%fused_computation.11 | loop fusion | flops 7864320 | bytes 10500096 | tf_op jit(solution)/shard_map/convert_element_type | solution.py:93
  77.5 0.0 copy-start.3
  77.5 7.4 %fusion.39 = f32[8,5,256,128]{3,2,1,0:T(8,128)} fusion(bf16[8,5,256,256]{3,2,1,0:T(8,128)(2,1)} %copy-done.6, bf16[8,5,256,128]{3,2,1,0:T(8,128)(2,1)S(1)} %bitcast.99), kind=kOutput, calls=%fused_computation.65 | convolution fusion | flops 671088640 | bytes 13107200 | tf_op jit(solution)/shard_map/hnij,hnid->hnjd/dot_general | solution.py:115
  84.9 2.4 %convolution_bitcast_fusion = f32[8,5,128,128]{2,3,1,0:T(8,128)} fusion(bf16[8,5,256,128]{3,2,1,0:T(8,128)(2,1)S(1)} %bitcast.100, bf16[8,5,256,128]{3,2,1,0:T(8,128)(2,1)S(1)} %bitcast.98), kind=kOutput, calls=%fused_computation.24 | convolution fusion | flops 335544320 | bytes 7864320 | tf_op jit(solution)/shard_map/hnid,hnie->hnde/dot_general | solution.py:97
  87.3 0.0 copy-done.3
  87.3 3.9 %select_convert_fusion = bf16[8,5,256,256]{3,2,1,0:T(8,128)(2,1)} fusion(pred[256,256]{1,0:T(8,128)(4,1)S(1)} %iota_compare_fusion, bf16[8,5,256,128]{3,2,1,0:T(8,128)(2,1)S(1)} %bitcast.101, bf16[8,5,256,128]{3,2,1,0:T(8,128)(2,1)S(1)} %bitcast.111), kind=kOutput, calls=%fused_computation | convolution fusion | flops 676331520 | bytes 10551296 | tf_op jit(solution)/shard_map/hnid,hnjd->hnij/dot_general | solution.py:105
  91.2 4.7 %copy.29 = f32[8,5,128,128]{3,1,2,0:T(8,128)} copy(f32[8,5,128,128]{2,3,1,0:T(8,128)} %convolution_bitcast_fusion) | data formatting | bytes 5242880 | tf_op jit(solution)/shard_map/hnid,hnie->hnde/dot_general | solution.py:97
  95.9 5.2 %fusion.25 = f32[1,8,128,128]{3,0,2,1:T(1,128)S(1)} fusion(f32[8,5,128,128]{3,1,2,0:T(8,128)} %copy.29, f32[]{:T(128)} %bitcast.21, s32[5]{0:T(128)S(1)} %copy-done.16), kind=kOutput, calls=%fused_computation.49 | convolution fusion | flops 7864330 | bytes 3145752 | tf_op jit(solution)/shard_map/c,hcde->hde/dot_general | solution.py:101
  101.1 0.0 slice-start.1
  101.1 1.4 collective-permute-start.5
  102.5 0.0 copy-start.8
  102.5 4.2 %fusion.38 = f32[8,5,256,128]{3,2,1,0:T(8,128)S(1)} fusion(bf16[8,5,256,256]{3,2,1,0:T(8,128)(2,1)} %select_convert_fusion, bf16[8,5,256,128]{3,2,1,0:T(8,128)(2,1)S(1)} %bitcast.97), kind=kOutput, calls=%fused_computation.64 | convolution fusion | flops 671088640 | bytes 13107200 | tf_op jit(solution)/shard_map/hnij,hnid->hnjd/dot_general | solution.py:112
  106.8 0.0 copy-start.5
  106.8 1.5 fusion.37
  108.3 17.3 %collective-permute-done.5 = f32[8,128,128]{2,1,0:T(8,128)S(1)} collective-permute-done((f32[8,128,128]{2,1,0:T(8,128)S(1)}, f32[8,128,128]{2,1,0:T(8,128)S(1)}, u32[]{:S(2)}, u32[]{:S(2)}) %collective-permute-start.5) | collective-permute-done | bytes 524320 | tf_op jit(solution)/shard_map/ppermute | solution.py:17
  125.6 0.1 multiply_add_fusion.1
  125.6 0.0 copy-start.4
  125.6 0.0 copy-start.13
  125.6 1.8 %collective-permute-start.7 = (f32[8,128,128]{2,1,0:T(8,128)S(1)}, f32[8,128,128]{2,1,0:T(8,128)S(1)}, u32[]{:S(2)}, u32[]{:S(2)}) collective-permute-start(f32[8,128,128]{2,1,0:T(8,128)S(1)} %multiply_add_fusion.1), channel_id=1, source_target_pairs={{8,0},{12,4},{9,1},{13,5},{10,2},{14,6},{11,3},{15,7},{24,16},{28,... | collective-permute-start | bytes 1572872 | tf_op jit(solution)/shard_map/ppermute | solution.py:17
  127.5 0.0 slice-start.2
  127.5 2.2 %fusion.19 = f32[8,128,128,5]{2,3,1,0:T(8,128)S(1)} fusion(f32[8,5,128,128]{3,1,2,0:T(8,128)S(1)} %copy-done.5, f32[5]{0:T(128)S(1)} %convert_element_type.63), kind=kOutput, calls=%fused_computation.44 | convolution fusion | flops 39321676 | bytes 5242900 | tf_op jit(solution)/shard_map/bc,hcde->hbde/dot_general | solution.py:118
  129.7 0.0 copy-done.4
  129.7 0.0 copy-done.13
  129.7 0.0 slice-start.3
  129.7 2.4 %add_convert_fusion = bf16[8,5,256,128]{3,2,1,0:T(8,128)(2,1)} fusion(f32[8,5,256,128]{3,2,1,0:T(8,128)S(1)} %fusion.37, bf16[8,5,256,128]{3,2,1,0:T(8,128)(2,1)S(1)} %bitcast.102, bf16[8,5,128,128]{3,2,1,0:T(8,128)(2,1)S(1)} %copy-done.13), kind=kOutput, calls=%fused_computation.13 | convolution fusion | flops 338165760 | bytes 11796480 | tf_op jit(solution)/shard_map/hnie,hnde->hnid/dot_general | solution.py:124
  132.2 21.3 %collective-permute-done.7 = f32[8,128,128]{2,1,0:T(8,128)S(1)} collective-permute-done((f32[8,128,128]{2,1,0:T(8,128)S(1)}, f32[8,128,128]{2,1,0:T(8,128)S(1)}, u32[]{:S(2)}, u32[]{:S(2)}) %collective-permute-start.7) | collective-permute-done | bytes 524320 | tf_op jit(solution)/shard_map/ppermute | solution.py:17
  153.4 0.1 multiply_add_fusion
  153.5 0.6 fusion.10
  154.2 0.0 copy-start.11
  154.2 2.4 %fusion = bf16[8,5,256,128]{3,2,1,0:T(8,128)(2,1)} fusion(f32[8,5,256,128]{3,2,1,0:T(8,128)S(1)} %bitcast.114, bf16[8,5,256,128]{3,2,1,0:T(8,128)(2,1)S(1)} %bitcast.108, bf16[8,5,128,128]{3,2,1,0:T(8,128)(2,1)S(1)} %fusion.10), kind=kOutput, calls=%fused_computation.3 | convolution fusion | flops 338165760 | bytes 11796480 | tf_op jit(solution)/shard_map/hnid,hnde->hnie/dot_general | solution.py:130
  156.6 2.4 %fusion.1 = bf16[8,5,256,128]{3,2,1,0:T(8,128)(2,1)} fusion(f32[8,5,256,128]{3,2,1,0:T(8,128)S(1)} %fusion.38, bf16[8,5,128,128]{3,2,1,0:T(8,128)(2,1)S(1)} %fusion.10, bf16[8,5,256,128]{3,2,1,0:T(8,128)(2,1)S(1)} %bitcast.112), kind=kOutput, calls=%fused_computation.5 | convolution fusion | flops 338165760 | bytes 11796480 | tf_op jit(solution)/shard_map/hnie,hnde->hnid/dot_general | solution.py:127
  (31 shorter events, 0.2 us)
Async XLA Ops:
  0.6 27.8 %copy-start = (bf16[8,1280,128]{2,1,0:T(8,128)(2,1)S(1)}, bf16[8,1280,128]{2,1,0:T(8,128)(2,1)}, u32[]{:S(2)}) copy-start(bf16[8,1280,128]{2,1,0:T(8,128)(2,1)} %param.6) | copy-start | bytes 7864324
  2.0 52.4 %collective-permute-start.6 = (f32[]{:T(128)}, f32[]{:T(128)}, u32[]{:S(2)}, u32[]{:S(2)}) collective-permute-start(f32[]{:T(128)} %bitcast.21), channel_id=1, source_target_pairs={{8,0},{12,4},{9,1},{13,5},{10,2},{14,6},{11,3},{15,7},{24,16},{28,... | collective-permute-start | bytes 20 | tf_op jit(solution)/shard_map/ppermute | solution.py:17
  3.3 49.9 %collective-permute-start.4 = (f32[]{:T(128)}, f32[]{:T(128)}, u32[]{:S(2)}, u32[]{:S(2)}) collective-permute-start(f32[]{:T(128)} %bitcast.21), channel_id=1, source_target_pairs={{4,0},{8,4},{12,8},{5,1},{9,5},{13,9},{6,2},{10,6},{14,10},{7,3},{... | collective-permute-start | bytes 20 | tf_op jit(solution)/shard_map/ppermute | solution.py:17
  4.6 50.5 %collective-permute-start.2 = (f32[]{:T(128)}, f32[]{:T(128)}, u32[]{:S(2)}, u32[]{:S(2)}) collective-permute-start(f32[]{:T(128)} %bitcast.7), channel_id=1, source_target_pairs={{0,8},{4,12},{1,9},{5,13},{2,10},{6,14},{3,11},{7,15},{16,24},{20,... | collective-permute-start | bytes 20 | tf_op jit(solution)/shard_map/ppermute | solution.py:17
  12.2 23.7 %collective-permute-start = (f32[]{:T(128)}, f32[]{:T(128)}, u32[]{:S(2)}, u32[]{:S(2)}) collective-permute-start(f32[]{:T(128)} %bitcast.7), channel_id=1, source_target_pairs={{0,4},{4,8},{8,12},{1,5},{5,9},{9,13},{2,6},{6,10},{10,14},{3,7},{... | collective-permute-start | bytes 20 | tf_op jit(solution)/shard_map/ppermute | solution.py:17
  17.2 4.9 %copy-start.16 = (s32[5]{0:T(128)S(1)}, s32[5]{0:T(128)}, u32[]{:S(2)}) copy-start(s32[5]{0:T(128)} %param.11) | copy-start | bytes 64
  20.6 1.5 copy-start.2
  27.0 12.3 %collective-permute-start.1 = (f32[8,128,128]{2,1,0:T(8,128)}, f32[8,128,128]{2,1,0:T(8,128)S(1)}, u32[]{:S(2)}, u32[]{:S(2)}) collective-permute-start(f32[8,128,128]{2,1,0:T(8,128)} %bitcast.11), channel_id=1, source_target_pairs={{0,4},{4,8},{8,12},{1,5},{5,9},{9,13},{2,6},{6,10},{10,14},{3,7},{... | collective-permute-start | bytes 1572872 | tf_op jit(solution)/shard_map/ppermute | solution.py:17
  28.5 3.4 %copy-start.9 = (bf16[8,1280,128]{2,1,0:T(8,128)(2,1)S(1)}, bf16[8,1280,128]{2,1,0:T(8,128)(2,1)}, u32[]{:S(2)}) copy-start(bf16[8,1280,128]{2,1,0:T(8,128)(2,1)} %param.8) | copy-start | bytes 7864324
  31.9 4.0 %copy-start.6 = (bf16[8,5,256,256]{3,2,1,0:T(8,128)(2,1)}, bf16[8,5,256,256]{3,2,1,0:T(8,128)(2,1)S(1)}, u32[]{:S(2)}) copy-start(bf16[8,5,256,256]{3,2,1,0:T(8,128)(2,1)S(1)} %select_convert_fusion.1) | copy-start | bytes 15728644
  41.2 14.5 %collective-permute-start.3 = (f32[8,128,128]{2,1,0:T(8,128)}, f32[8,128,128]{2,1,0:T(8,128)}, u32[]{:S(2)}, u32[]{:S(2)}) collective-permute-start(f32[8,128,128]{2,1,0:T(8,128)} %multiply_add_fusion.3), channel_id=1, source_target_pairs={{0,8},{4,12},{1,9},{5,13},{2,10},{6,14},{3,11},{7,15},{16,24},{20,... | collective-permute-start | bytes 1572872 | tf_op jit(solution)/shard_map/ppermute | solution.py:17
  55.8 3.7 %copy-start.7 = (f32[8,5,256,128]{3,2,1,0:T(8,128)S(1)}, f32[8,5,256,128]{3,2,1,0:T(8,128)}, u32[]{:S(2)}) copy-start(f32[8,5,256,128]{3,2,1,0:T(8,128)} %fusion.35) | copy-start | bytes 15728644
  59.5 1.2 copy-start.12
  59.5 2.3 %copy-start.14 = (bf16[8,1280,128]{2,1,0:T(8,128)(2,1)S(1)}, bf16[8,1280,128]{2,1,0:T(8,128)(2,1)}, u32[]{:S(2)}) copy-start(bf16[8,1280,128]{2,1,0:T(8,128)(2,1)} %param.9) | copy-start | bytes 7864324
  59.5 2.3 %copy-start.15 = (f32[8,128]{1,0:T(8,128)S(1)}, f32[8,128]{1,0:T(8,128)}, u32[]{:S(2)}) copy-start(f32[8,128]{1,0:T(8,128)} %param.10) | copy-start | bytes 12292
  60.7 2.4 %copy-start.1 = (f32[8,5,256,128]{3,2,1,0:T(8,128)}, f32[8,5,256,128]{3,2,1,0:T(8,128)S(1)}, u32[]{:S(2)}) copy-start(f32[8,5,256,128]{3,2,1,0:T(8,128)S(1)} %get-tuple-element.10) | copy-start | bytes 15728644
  77.5 9.8 %copy-start.3 = (bf16[8,1280,128]{2,1,0:T(8,128)(2,1)}, bf16[8,1280,128]{2,1,0:T(8,128)(2,1)S(1)}, u32[]{:S(2)}) copy-start(bf16[8,1280,128]{2,1,0:T(8,128)(2,1)S(1)} %fusion.5) | copy-start | bytes 7864324
  84.9 2.4 %copy-start.10 = (bf16[8,1280,128]{2,1,0:T(8,128)(2,1)S(1)}, bf16[8,1280,128]{2,1,0:T(8,128)(2,1)}, u32[]{:S(2)}) copy-start(bf16[8,1280,128]{2,1,0:T(8,128)(2,1)} %param.8) | copy-start | bytes 7864324
  95.9 10.9 %slice-start = ((s8[5242880]{0:T(1024)(128)(4,1)}), s8[4194304]{0:T(1024)(128)(4,1)S(1)}, s32[]{:S(2)}) async-start(s8[5242880]{0:T(1024)(128)(4,1)} %bitcast.103), calls=%async_computation | async-start | bytes 8388608
  101.1 5.7 %slice-start.1 = ((s8[5242880]{0:T(1024)(128)(4,1)}), s8[1048576]{0:T(1024)(128)(4,1)S(1)}, s32[]{:S(2)}) async-start(s8[5242880]{0:T(1024)(128)(4,1)} %bitcast.103), calls=%async_computation.1 | async-start | bytes 2097152
  101.1 24.5 %collective-permute-start.5 = (f32[8,128,128]{2,1,0:T(8,128)S(1)}, f32[8,128,128]{2,1,0:T(8,128)S(1)}, u32[]{:S(2)}, u32[]{:S(2)}) collective-permute-start(f32[8,128,128]{2,1,0:T(8,128)S(1)} %bitcast.118), channel_id=1, source_target_pairs={{4,0},{8,4},{12,8},{5,1},{9,5},{13,9},{6,2},{10,6},{14,10},{7,3},{... | collective-permute-start | bytes 1572872 | tf_op jit(solution)/shard_map/ppermute | solution.py:17
  102.5 4.2 %copy-start.8 = (bf16[8,1280,128]{2,1,0:T(8,128)(2,1)S(1)}, bf16[8,1280,128]{2,1,0:T(8,128)(2,1)}, u32[]{:S(2)}) copy-start(bf16[8,1280,128]{2,1,0:T(8,128)(2,1)} %param.7) | copy-start | bytes 7864324
  106.8 20.7 %copy-start.5 = (f32[8,5,128,128]{3,1,2,0:T(8,128)S(1)}, f32[8,5,128,128]{3,1,2,0:T(8,128)}, u32[]{:S(2)}) copy-start(f32[8,5,128,128]{3,1,2,0:T(8,128)} %copy.29) | copy-start | bytes 7864324
  125.6 4.1 %copy-start.4 = (bf16[8,1280,128]{2,1,0:T(8,128)(2,1)S(1)}, bf16[8,1280,128]{2,1,0:T(8,128)(2,1)}, u32[]{:S(2)}) copy-start(bf16[8,1280,128]{2,1,0:T(8,128)(2,1)} %copy-done.3) | copy-start | bytes 7864324
  125.6 4.1 %copy-start.13 = (bf16[8,5,128,128]{3,2,1,0:T(8,128)(2,1)S(1)}, bf16[8,5,128,128]{3,2,1,0:T(8,128)(2,1)}, u32[]{:S(2)}) copy-start(bf16[8,5,128,128]{3,2,1,0:T(8,128)(2,1)} %copy-done.12) | copy-start | bytes 3932164
  125.6 27.8 %collective-permute-start.7 = (f32[8,128,128]{2,1,0:T(8,128)S(1)}, f32[8,128,128]{2,1,0:T(8,128)S(1)}, u32[]{:S(2)}, u32[]{:S(2)}) collective-permute-start(f32[8,128,128]{2,1,0:T(8,128)S(1)} %multiply_add_fusion.1), channel_id=1, source_target_pairs={{8,0},{12,4},{9,1},{13,5},{10,2},{14,6},{11,3},{15,7},{24,16},{28,... | collective-permute-start | bytes 1572872 | tf_op jit(solution)/shard_map/ppermute | solution.py:17
  127.5 26.7 %slice-start.2 = ((s8[5242880]{0:T(1024)(128)(4,1)}), s8[4194304]{0:T(1024)(128)(4,1)S(1)}, s32[]{:S(2)}) async-start(s8[5242880]{0:T(1024)(128)(4,1)} %bitcast.113), calls=%async_computation.2 | async-start | bytes 8388608
  129.7 24.5 %slice-start.3 = ((s8[5242880]{0:T(1024)(128)(4,1)}), s8[1048576]{0:T(1024)(128)(4,1)S(1)}, s32[]{:S(2)}) async-start(s8[5242880]{0:T(1024)(128)(4,1)} %bitcast.113), calls=%async_computation.3 | async-start | bytes 2097152
  154.2 2.4 %copy-start.11 = (bf16[8,1280,128]{2,1,0:T(8,128)(2,1)S(1)}, bf16[8,1280,128]{2,1,0:T(8,128)(2,1)}, u32[]{:S(2)}) copy-start(bf16[8,1280,128]{2,1,0:T(8,128)(2,1)} %param.8) | copy-start | bytes 7864324
where the time goes:
time: 160 us; the launch traced here: 159 us
  matrix products  58.1 us (36%)
  waiting for transfers between devices  40.7 us (25%)
  starting transfers between devices  24.5 us (15%)
  other arithmetic  11.4 us (7%)
  blocking collectives  10.3 us (6%)
  local copies, waits for them, and re-layouts  9.19 us (6%)
  between operations  4.79 us (3%)
    ppermute x8, waiting for transfers between devices, shift(): return lax.ppermute(value, axis, pairs)  40.7 us
    ppermute x8, starting transfers between devices, shift(): return lax.ppermute(value, axis, pairs)  24.5 us
    psum x1, blocking collectives, on_device(): total_sums = lax.psum(local_sums, ('sub', 'head'))  10.3 us
    dot_general x1, matrix products, on_device(): jnp.einsum('hnij,hnid->hnjd', block_probs, output_grad_blocks, preferred_...  7.37 us
    dot_general x1, matrix products, on_device(): jnp.einsum('bc,hcde->hbde', earlier_mask, key_value_block, precision=high...  7.22 us
    dot_general x1, matrix products, on_device(): jnp.einsum('c,hcde->hde', first_match, query_grad_block, precision=highes...  5.18 us
    dot_general x1, matrix products, on_device(): jnp.einsum('c,hcde->hde', last_match, key_value_block, precision=highest_...  4.89 us
    dot_general x1, local copies, waits for them, and re-layouts, on_device(): jnp.einsum('hnid,hnie->hnde', query_blocks, output_grad_blocks, preferred...  4.7 us
  transfers between devices with their start and end apart: 8, of which 3 were waited for; matrix products, arithmetic and copies ran while one was open for 22% of the time, Pallas kernels for 0%

commit v1 on v0

--- a/solution.py
+++ b/solution.py
@@ -86,7 +86,9 @@
     local_sums = jnp.stack(
         [jnp.sum(raw_attn * raw_attn, axis=(0, 2)), jnp.sum(scaled * raw_attn, axis=(0, 2))]
     )
-    total_sums = lax.psum(local_sums, ("sub", "head"))
+    total_sums = local_sums
+    for mesh_axis in ("head", "sub"):
+        total_sums = lax.psum(total_sums, mesh_axis)
     root_mean = jnp.sqrt(total_sums[0] / feature_count + 1e-06)
     inner_mean = total_sums[1] / feature_count
     factor = inner_mean / (root_mean * root_mean)

time: 160 us -> 158 us (0.988)
  waiting for transfers between devices: 40.7 us -> 37.6 us
  blocking collectives: 10.3 us -> 12 us
    ppermute x8, waiting for transfers between devices: 40.7 us -> 37.6 us  [shift(): return lax.ppermute(value, axis, pairs)]
    psum x1 -> x2, blocking collectives: 10.3 us -> 12 us  [on_device(): total_sums = lax.psum(total_sums, mesh_axis)]
where the time goes in v1:
time: 158 us
  matrix products  58.1 us (37%)
  waiting for transfers between devices  37.6 us (24%)
  starting transfers between devices  24.5 us (16%)
  blocking collectives  12 us (8%)
  other arithmetic  11.4 us (7%)
  local copies, waits for them, and re-layouts  9.18 us (6%)
  between operations  4.72 us (3%)
    ppermute x8, waiting for transfers between devices, shift(): return lax.ppermute(value, axis, pairs)  37.6 us
    ppermute x8, starting transfers between devices, shift(): return lax.ppermute(value, axis, pairs)  24.5 us
    psum x2, blocking collectives, on_device(): total_sums = lax.psum(total_sums, mesh_axis)  12 us
    dot_general x1, matrix products, on_device(): jnp.einsum('hnij,hnid->hnjd', block_probs, output_grad_blocks, preferred_...  7.37 us
    dot_general x1, matrix products, on_device(): jnp.einsum('bc,hcde->hbde', earlier_mask, key_value_block, precision=high...  7.21 us
    dot_general x1, matrix products, on_device(): jnp.einsum('c,hcde->hde', first_match, query_grad_block, precision=highes...  5.19 us
    dot_general x1, matrix products, on_device(): jnp.einsum('c,hcde->hde', last_match, key_value_block, precision=highest_...  4.89 us
    dot_general x1, local copies, waits for them, and re-layouts, on_device(): jnp.einsum('hnid,hnie->hnde', query_blocks, output_grad_blocks, preferred...  4.68 us
  transfers between devices with their start and end apart: 8, of which 3 were waited for; matrix products, arithmetic and copies ran while one was open for 22% of the time, Pallas kernels for 0%

profile of v1, /device:TPU:0, one launch (start us, length us, event | category | flops | bytes accessed | tf_op | source)
XLA Modules:
  0.0 157.5 jit_solution(15554806018053834539)
XLA Ops:
  0.6 0.0 copy-start
  0.6 0.8 convert_element_type.63
  1.5 0.6 fusion.34
  2.0 1.3 collective-permute-start.6
  3.3 1.3 collective-permute-start.4
  4.6 7.6 %collective-permute-start.2 = (f32[]{:T(128)}, f32[]{:T(128)}, u32[]{:S(2)}, u32[]{:S(2)}) collective-permute-start(f32[]{:T(128)} %bitcast.7), channel_id=1, source_target_pairs={{0,8},{4,12},{1,9},{5,13},{2,10},{6,14},{3,11},{7,15},{16,24},{20,... | collective-permute-start | bytes 20 | tf_op jit(solution)/shard_map/ppermute | solution.py:17
  12.2 4.9 %collective-permute-start = (f32[]{:T(128)}, f32[]{:T(128)}, u32[]{:S(2)}, u32[]{:S(2)}) collective-permute-start(f32[]{:T(128)} %bitcast.7), channel_id=1, source_target_pairs={{0,4},{4,8},{8,12},{1,5},{5,9},{9,13},{2,6},{6,10},{10,14},{3,7},{... | collective-permute-start | bytes 20 | tf_op jit(solution)/shard_map/ppermute | solution.py:17
  17.1 3.4 %fusion.36 = f32[8,5,128,128]{3,2,1,0:T(8,128)S(1)} fusion(bf16[8,5,256,128]{3,2,1,0:T(8,128)(2,1)} %bitcast.105, bf16[8,5,256,128]{3,2,1,0:T(8,128)(2,1)} %bitcast.109), kind=kOutput, calls=%fused_computation.62 | convolution fusion | flops 335544320 | bytes 7864320 | tf_op jit(solution)/shard_map/hnid,hnie->hnde/dot_general | solution.py:61
  20.5 0.0 copy-start.2
  20.5 1.5 copy-done.2
  22.0 4.9 %fusion.6 = f32[1,8,128,128]{3,0,2,1:T(1,128)} fusion(f32[8,5,128,128]{3,2,1,0:T(8,128)S(1)} %fusion.36, f32[]{:T(128)} %bitcast.7, s32[5]{0:T(128)S(1)} %copy-done.16), kind=kOutput, calls=%fused_computation.16 | convolution fusion | flops 7864330 | bytes 3145752 | tf_op jit(solution)/shard_map/c,hcde->hde/dot_general | solution.py:65
  26.9 1.4 collective-permute-start.1
  28.4 0.0 copy-start.9
  28.4 3.4 %select_convert_fusion.1 = bf16[8,5,256,256]{3,2,1,0:T(8,128)(2,1)S(1)} fusion(pred[256,256]{1,0:T(8,128)(4,1)S(1)} %iota_compare_fusion, bf16[8,5,256,128]{3,2,1,0:T(8,128)(2,1)S(1)} %bitcast.95, bf16[8,5,256,128]{3,2,1,0:T(8,128)(2,1)} %bitcast.106), kind=kOutput, calls=%fused_computation.1 | convolution fusion | flops 676331520 | bytes 10551296 | tf_op jit(solution)/shard_map/hnid,hnjd->hnij/dot_general | solution.py:67
  31.9 0.0 copy-done.9
  31.9 0.0 copy-start.6
  31.9 4.0 %fusion.35 = f32[8,5,256,128]{3,2,1,0:T(8,128)} fusion(bf16[8,5,256,256]{3,2,1,0:T(8,128)(2,1)S(1)} %select_convert_fusion.1, bf16[8,5,256,128]{3,2,1,0:T(8,128)(2,1)S(1)} %bitcast.110), kind=kOutput, calls=%fused_computation.61 | convolution fusion | flops 671088640 | bytes 13107200 | tf_op jit(solution)/shard_map/hnij,hnjd->hnid/dot_general | solution.py:71
  35.9 0.0 collective-permute-done
  37.1 2.2 %collective-permute-done.1 = f32[8,128,128]{2,1,0:T(8,128)S(1)} collective-permute-done((f32[8,128,128]{2,1,0:T(8,128)}, f32[8,128,128]{2,1,0:T(8,128)S(1)}, u32[]{:S(2)}, u32[]{:S(2)}) %collective-permute-start.1) | collective-permute-done | bytes 524320 | tf_op jit(solution)/shard_map/ppermute | solution.py:17
  39.3 1.9 %multiply_add_fusion.3 = f32[8,128,128]{2,1,0:T(8,128)} fusion(f32[8,128,128]{2,1,0:T(8,128)} %bitcast.11, f32[8,128,128]{2,1,0:T(8,128)S(1)} %collective-permute-done.1, f32[]{:T(128)S(6)} %convert_element_type.66, pred[]{:T(512)S(6)} %ge.12), kind=kLoop, calls=%fused_computation.28 | loop fusion | flops 393216 | bytes 1572869 | tf_op jit(solution)/shard_map/add | solution.py:21
  41.2 4.8 %collective-permute-start.3 = (f32[8,128,128]{2,1,0:T(8,128)}, f32[8,128,128]{2,1,0:T(8,128)}, u32[]{:S(2)}, u32[]{:S(2)}) collective-permute-start(f32[8,128,128]{2,1,0:T(8,128)} %multiply_add_fusion.3), channel_id=1, source_target_pairs={{0,8},{4,12},{1,9},{5,13},{2,10},{6,14},{3,11},{7,15},{16,24},{20,... | collective-permute-start | bytes 1572872 | tf_op jit(solution)/shard_map/ppermute | solution.py:17
  46.0 7.2 %fusion.8 = f32[8,128,128,5]{2,3,1,0:T(8,128)} fusion(f32[8,5,128,128]{3,2,1,0:T(8,128)} %copy-done.2, f32[5]{0:T(128)S(1)} %convert_element_type.63), kind=kOutput, calls=%fused_computation.18 | convolution fusion | flops 39321676 | bytes 5242900 | tf_op jit(solution)/shard_map/bc,hcde->hbde/dot_general | solution.py:74
  53.2 0.0 collective-permute-done.4
  54.4 0.0 collective-permute-done.6
  55.1 0.0 collective-permute-done.2
  55.6 0.0 collective-permute-done.3
  55.7 0.1 multiply_add_fusion.2
  55.8 0.0 copy-start.7
  55.8 3.0 %fusion.11 = bf16[8,5,128,128]{3,2,1,0:T(8,128)(2,1)S(1)} fusion(f32[8,128,128,5]{2,3,1,0:T(8,128)} %fusion.8, f32[8,128,128]{2,1,0:T(8,128)S(1)} %multiply_add_fusion.2, f32[5]{0:T(128)S(1)} %get-tuple-element.6), kind=kLoop, calls=%fused_computation.23 | loop fusion | flops 1966080 | bytes 4456468 | tf_op jit(solution)/shard_map/convert_element_type | solution.py:79
  58.7 0.8 copy-done.7
  59.5 1.2 multiply_reduce_fusion
  60.7 1.1 copy-done.14
  61.8 0.8 fusion.2
  62.6 0.5 copy-done.1
  63.1 3.3 %psum.14 = f32[2,1280]{1,0:T(2,128)S(1)} all-reduce(f32[2,1280]{1,0:T(2,128)S(1)} %pad_maximum_fusion), channel_id=1, replica_groups=mesh['groups'=2,'ctx'=4,'sub'=2,'head'=2] {'head'}, use_global_device_ids=true, to_apply=%region_2.3 | all-reduce | flops 2560 | bytes 20480 | tf_op jit(solution)/shard_map/psum | solution.py:91
  66.4 8.7 %psum.15 = f32[2,1280]{1,0:T(2,128)S(1)} all-reduce(f32[2,1280]{1,0:T(2,128)S(1)} %psum.14), channel_id=1, replica_groups=mesh['groups'=2,'ctx'=4,'sub'=2,'head'=2] {'sub'}, use_global_device_ids=true, to_apply=%region_3.4 | all-reduce | flops 2560 | bytes 20480 | tf_op jit(solution)/shard_map/psum | solution.py:91
  75.2 4.0 %fusion.5 = bf16[8,1280,128]{2,1,0:T(8,128)(2,1)S(1)} fusion(f32[8,5,256,128]{3,2,1,0:T(8,128)} %copy-done.1, bf16[8,1280,128]{2,1,0:T(8,128)(2,1)} %param.9, f32[1280]{0:T(1024)S(1)} %get-tuple-element.4, f32[1280]{0:T(1024)S(1)} %multiply_divide_fusion, f32[8,128]{1,0:T(8,128)S(1)} %copy-done.15), kind=kLoop, calls=%fused_computation.11 | loop fusion | flops 7864320 | bytes 10500096 | tf_op jit(solution)/shard_map/convert_element_type | solution.py:95
  79.2 0.0 copy-start.3
  79.2 7.4 %fusion.39 = f32[8,5,256,128]{3,2,1,0:T(8,128)} fusion(bf16[8,5,256,256]{3,2,1,0:T(8,128)(2,1)} %copy-done.6, bf16[8,5,256,128]{3,2,1,0:T(8,128)(2,1)S(1)} %bitcast.99), kind=kOutput, calls=%fused_computation.65 | convolution fusion | flops 671088640 | bytes 13107200 | tf_op jit(solution)/shard_map/hnij,hnid->hnjd/dot_general | solution.py:117
  86.6 2.4 %convolution_bitcast_fusion = f32[8,5,128,128]{2,3,1,0:T(8,128)} fusion(bf16[8,5,256,128]{3,2,1,0:T(8,128)(2,1)S(1)} %bitcast.100, bf16[8,5,256,128]{3,2,1,0:T(8,128)(2,1)S(1)} %bitcast.98), kind=kOutput, calls=%fused_computation.24 | convolution fusion | flops 335544320 | bytes 7864320 | tf_op jit(solution)/shard_map/hnid,hnie->hnde/dot_general | solution.py:99
  89.0 3.8 %select_convert_fusion = bf16[8,5,256,256]{3,2,1,0:T(8,128)(2,1)} fusion(pred[256,256]{1,0:T(8,128)(4,1)S(1)} %iota_compare_fusion, bf16[8,5,256,128]{3,2,1,0:T(8,128)(2,1)S(1)} %bitcast.101, bf16[8,5,256,128]{3,2,1,0:T(8,128)(2,1)S(1)} %bitcast.111), kind=kOutput, calls=%fused_computation | convolution fusion | flops 676331520 | bytes 10551296 | tf_op jit(solution)/shard_map/hnid,hnjd->hnij/dot_general | solution.py:107
  92.8 4.7 %copy.29 = f32[8,5,128,128]{3,1,2,0:T(8,128)} copy(f32[8,5,128,128]{2,3,1,0:T(8,128)} %convolution_bitcast_fusion) | data formatting | bytes 5242880 | tf_op jit(solution)/shard_map/hnid,hnie->hnde/dot_general | solution.py:99
  97.5 5.2 %fusion.25 = f32[1,8,128,128]{3,0,2,1:T(1,128)S(1)} fusion(f32[8,5,128,128]{3,1,2,0:T(8,128)} %copy.29, f32[]{:T(128)} %bitcast.21, s32[5]{0:T(128)S(1)} %copy-done.16), kind=kOutput, calls=%fused_computation.49 | convolution fusion | flops 7864330 | bytes 3145752 | tf_op jit(solution)/shard_map/c,hcde->hde/dot_general | solution.py:103
  102.7 0.0 slice-start.1
  102.7 1.4 collective-permute-start.5
  104.1 0.0 copy-start.8
  104.1 4.2 %fusion.38 = f32[8,5,256,128]{3,2,1,0:T(8,128)S(1)} fusion(bf16[8,5,256,256]{3,2,1,0:T(8,128)(2,1)} %select_convert_fusion, bf16[8,5,256,128]{3,2,1,0:T(8,128)(2,1)S(1)} %bitcast.97), kind=kOutput, calls=%fused_computation.64 | convolution fusion | flops 671088640 | bytes 13107200 | tf_op jit(solution)/shard_map/hnij,hnid->hnjd/dot_general | solution.py:114
  108.4 1.5 fusion.37
  109.9 15.6 %collective-permute-done.5 = f32[8,128,128]{2,1,0:T(8,128)S(1)} collective-permute-done((f32[8,128,128]{2,1,0:T(8,128)S(1)}, f32[8,128,128]{2,1,0:T(8,128)S(1)}, u32[]{:S(2)}, u32[]{:S(2)}) %collective-permute-start.5) | collective-permute-done | bytes 524320 | tf_op jit(solution)/shard_map/ppermute | solution.py:17
  125.5 0.1 multiply_add_fusion.1
  125.6 0.0 copy-start.4
  125.6 0.0 copy-start.13
  125.6 1.8 %collective-permute-start.7 = (f32[8,128,128]{2,1,0:T(8,128)S(1)}, f32[8,128,128]{2,1,0:T(8,128)S(1)}, u32[]{:S(2)}, u32[]{:S(2)}) collective-permute-start(f32[8,128,128]{2,1,0:T(8,128)S(1)} %multiply_add_fusion.1), channel_id=1, source_target_pairs={{8,0},{12,4},{9,1},{13,5},{10,2},{14,6},{11,3},{15,7},{24,16},{28,... | collective-permute-start | bytes 1572872 | tf_op jit(solution)/shard_map/ppermute | solution.py:17
  127.4 0.0 copy-done.5
  127.4 0.0 slice-start.2
  127.4 2.2 %fusion.19 = f32[8,128,128,5]{2,3,1,0:T(8,128)S(1)} fusion(f32[8,5,128,128]{3,1,2,0:T(8,128)S(1)} %copy-done.5, f32[5]{0:T(128)S(1)} %convert_element_type.63), kind=kOutput, calls=%fused_computation.44 | convolution fusion | flops 39321676 | bytes 5242900 | tf_op jit(solution)/shard_map/bc,hcde->hbde/dot_general | solution.py:120
  129.7 0.0 slice-start.3
  129.7 2.4 %add_convert_fusion = bf16[8,5,256,128]{3,2,1,0:T(8,128)(2,1)} fusion(f32[8,5,256,128]{3,2,1,0:T(8,128)S(1)} %fusion.37, bf16[8,5,256,128]{3,2,1,0:T(8,128)(2,1)S(1)} %bitcast.102, bf16[8,5,128,128]{3,2,1,0:T(8,128)(2,1)S(1)} %copy-done.13), kind=kOutput, calls=%fused_computation.13 | convolution fusion | flops 338165760 | bytes 11796480 | tf_op jit(solution)/shard_map/hnie,hnde->hnid/dot_general | solution.py:126
  132.1 19.8 %collective-permute-done.7 = f32[8,128,128]{2,1,0:T(8,128)S(1)} collective-permute-done((f32[8,128,128]{2,1,0:T(8,128)S(1)}, f32[8,128,128]{2,1,0:T(8,128)S(1)}, u32[]{:S(2)}, u32[]{:S(2)}) %collective-permute-start.7) | collective-permute-done | bytes 524320 | tf_op jit(solution)/shard_map/ppermute | solution.py:17
  151.9 0.1 multiply_add_fusion
  152.0 0.6 fusion.10
  152.7 0.0 copy-start.11
  152.7 2.4 %fusion = bf16[8,5,256,128]{3,2,1,0:T(8,128)(2,1)} fusion(f32[8,5,256,128]{3,2,1,0:T(8,128)S(1)} %bitcast.114, bf16[8,5,256,128]{3,2,1,0:T(8,128)(2,1)S(1)} %bitcast.108, bf16[8,5,128,128]{3,2,1,0:T(8,128)(2,1)S(1)} %fusion.10), kind=kOutput, calls=%fused_computation.3 | convolution fusion | flops 338165760 | bytes 11796480 | tf_op jit(solution)/shard_map/hnid,hnde->hnie/dot_general | solution.py:132
  155.1 2.4 %fusion.1 = bf16[8,5,256,128]{3,2,1,0:T(8,128)(2,1)} fusion(f32[8,5,256,128]{3,2,1,0:T(8,128)S(1)} %fusion.38, bf16[8,5,128,128]{3,2,1,0:T(8,128)(2,1)S(1)} %fusion.10, bf16[8,5,256,128]{3,2,1,0:T(8,128)(2,1)S(1)} %bitcast.112), kind=kOutput, calls=%fused_computation.5 | convolution fusion | flops 338165760 | bytes 11796480 | tf_op jit(solution)/shard_map/hnie,hnde->hnid/dot_general | solution.py:129
  (32 shorter events, 0.2 us)
Async XLA Ops:
  0.6 27.8 %copy-start = (bf16[8,1280,128]{2,1,0:T(8,128)(2,1)S(1)}, bf16[8,1280,128]{2,1,0:T(8,128)(2,1)}, u32[]{:S(2)}) copy-start(bf16[8,1280,128]{2,1,0:T(8,128)(2,1)} %param.6) | copy-start | bytes 7864324
  2.0 52.4 %collective-permute-start.6 = (f32[]{:T(128)}, f32[]{:T(128)}, u32[]{:S(2)}, u32[]{:S(2)}) collective-permute-start(f32[]{:T(128)} %bitcast.21), channel_id=1, source_target_pairs={{8,0},{12,4},{9,1},{13,5},{10,2},{14,6},{11,3},{15,7},{24,16},{28,... | collective-permute-start | bytes 20 | tf_op jit(solution)/shard_map/ppermute | solution.py:17
  3.3 49.8 %collective-permute-start.4 = (f32[]{:T(128)}, f32[]{:T(128)}, u32[]{:S(2)}, u32[]{:S(2)}) collective-permute-start(f32[]{:T(128)} %bitcast.21), channel_id=1, source_target_pairs={{4,0},{8,4},{12,8},{5,1},{9,5},{13,9},{6,2},{10,6},{14,10},{7,3},{... | collective-permute-start | bytes 20 | tf_op jit(solution)/shard_map/ppermute | solution.py:17
  4.6 50.4 %collective-permute-start.2 = (f32[]{:T(128)}, f32[]{:T(128)}, u32[]{:S(2)}, u32[]{:S(2)}) collective-permute-start(f32[]{:T(128)} %bitcast.7), channel_id=1, source_target_pairs={{0,8},{4,12},{1,9},{5,13},{2,10},{6,14},{3,11},{7,15},{16,24},{20,... | collective-permute-start | bytes 20 | tf_op jit(solution)/shard_map/ppermute | solution.py:17
  12.2 23.7 %collective-permute-start = (f32[]{:T(128)}, f32[]{:T(128)}, u32[]{:S(2)}, u32[]{:S(2)}) collective-permute-start(f32[]{:T(128)} %bitcast.7), channel_id=1, source_target_pairs={{0,4},{4,8},{8,12},{1,5},{5,9},{9,13},{2,6},{6,10},{10,14},{3,7},{... | collective-permute-start | bytes 20 | tf_op jit(solution)/shard_map/ppermute | solution.py:17
  17.1 4.9 %copy-start.16 = (s32[5]{0:T(128)S(1)}, s32[5]{0:T(128)}, u32[]{:S(2)}) copy-start(s32[5]{0:T(128)} %param.11) | copy-start | bytes 64
  20.5 1.5 copy-start.2
  26.9 12.3 %collective-permute-start.1 = (f32[8,128,128]{2,1,0:T(8,128)}, f32[8,128,128]{2,1,0:T(8,128)S(1)}, u32[]{:S(2)}, u32[]{:S(2)}) collective-permute-start(f32[8,128,128]{2,1,0:T(8,128)} %bitcast.11), channel_id=1, source_target_pairs={{0,4},{4,8},{8,12},{1,5},{5,9},{9,13},{2,6},{6,10},{10,14},{3,7},{... | collective-permute-start | bytes 1572872 | tf_op jit(solution)/shard_map/ppermute | solution.py:17
  28.4 3.4 %copy-start.9 = (bf16[8,1280,128]{2,1,0:T(8,128)(2,1)S(1)}, bf16[8,1280,128]{2,1,0:T(8,128)(2,1)}, u32[]{:S(2)}) copy-start(bf16[8,1280,128]{2,1,0:T(8,128)(2,1)} %param.8) | copy-start | bytes 7864324
  31.9 4.0 %copy-start.6 = (bf16[8,5,256,256]{3,2,1,0:T(8,128)(2,1)}, bf16[8,5,256,256]{3,2,1,0:T(8,128)(2,1)S(1)}, u32[]{:S(2)}) copy-start(bf16[8,5,256,256]{3,2,1,0:T(8,128)(2,1)S(1)} %select_convert_fusion.1) | copy-start | bytes 15728644
  41.2 14.5 %collective-permute-start.3 = (f32[8,128,128]{2,1,0:T(8,128)}, f32[8,128,128]{2,1,0:T(8,128)}, u32[]{:S(2)}, u32[]{:S(2)}) collective-permute-start(f32[8,128,128]{2,1,0:T(8,128)} %multiply_add_fusion.3), channel_id=1, source_target_pairs={{0,8},{4,12},{1,9},{5,13},{2,10},{6,14},{3,11},{7,15},{16,24},{20,... | collective-permute-start | bytes 1572872 | tf_op jit(solution)/shard_map/ppermute | solution.py:17
  55.8 3.7 %copy-start.7 = (f32[8,5,256,128]{3,2,1,0:T(8,128)S(1)}, f32[8,5,256,128]{3,2,1,0:T(8,128)}, u32[]{:S(2)}) copy-start(f32[8,5,256,128]{3,2,1,0:T(8,128)} %fusion.35) | copy-start | bytes 15728644
  59.5 1.2 copy-start.12
  59.5 2.3 %copy-start.14 = (bf16[8,1280,128]{2,1,0:T(8,128)(2,1)S(1)}, bf16[8,1280,128]{2,1,0:T(8,128)(2,1)}, u32[]{:S(2)}) copy-start(bf16[8,1280,128]{2,1,0:T(8,128)(2,1)} %param.9) | copy-start | bytes 7864324
  59.5 2.3 %copy-start.15 = (f32[8,128]{1,0:T(8,128)S(1)}, f32[8,128]{1,0:T(8,128)}, u32[]{:S(2)}) copy-start(f32[8,128]{1,0:T(8,128)} %param.10) | copy-start | bytes 12292
  60.7 2.4 %copy-start.1 = (f32[8,5,256,128]{3,2,1,0:T(8,128)}, f32[8,5,256,128]{3,2,1,0:T(8,128)S(1)}, u32[]{:S(2)}) copy-start(f32[8,5,256,128]{3,2,1,0:T(8,128)S(1)} %get-tuple-element.10) | copy-start | bytes 15728644
  79.2 9.8 %copy-start.3 = (bf16[8,1280,128]{2,1,0:T(8,128)(2,1)}, bf16[8,1280,128]{2,1,0:T(8,128)(2,1)S(1)}, u32[]{:S(2)}) copy-start(bf16[8,1280,128]{2,1,0:T(8,128)(2,1)S(1)} %fusion.5) | copy-start | bytes 7864324
  86.6 2.4 %copy-start.10 = (bf16[8,1280,128]{2,1,0:T(8,128)(2,1)S(1)}, bf16[8,1280,128]{2,1,0:T(8,128)(2,1)}, u32[]{:S(2)}) copy-start(bf16[8,1280,128]{2,1,0:T(8,128)(2,1)} %param.8) | copy-start | bytes 7864324
  97.5 10.9 %slice-start = ((s8[5242880]{0:T(1024)(128)(4,1)}), s8[4194304]{0:T(1024)(128)(4,1)S(1)}, s32[]{:S(2)}) async-start(s8[5242880]{0:T(1024)(128)(4,1)} %bitcast.103), calls=%async_computation | async-start | bytes 8388608
  102.7 5.7 %slice-start.1 = ((s8[5242880]{0:T(1024)(128)(4,1)}), s8[1048576]{0:T(1024)(128)(4,1)S(1)}, s32[]{:S(2)}) async-start(s8[5242880]{0:T(1024)(128)(4,1)} %bitcast.103), calls=%async_computation.1 | async-start | bytes 2097152
  102.7 22.8 %collective-permute-start.5 = (f32[8,128,128]{2,1,0:T(8,128)S(1)}, f32[8,128,128]{2,1,0:T(8,128)S(1)}, u32[]{:S(2)}, u32[]{:S(2)}) collective-permute-start(f32[8,128,128]{2,1,0:T(8,128)S(1)} %bitcast.118), channel_id=1, source_target_pairs={{4,0},{8,4},{12,8},{5,1},{9,5},{13,9},{6,2},{10,6},{14,10},{7,3},{... | collective-permute-start | bytes 1572872 | tf_op jit(solution)/shard_map/ppermute | solution.py:17
  104.1 4.2 %copy-start.8 = (bf16[8,1280,128]{2,1,0:T(8,128)(2,1)S(1)}, bf16[8,1280,128]{2,1,0:T(8,128)(2,1)}, u32[]{:S(2)}) copy-start(bf16[8,1280,128]{2,1,0:T(8,128)(2,1)} %param.7) | copy-start | bytes 7864324
  108.4 19.0 %copy-start.5 = (f32[8,5,128,128]{3,1,2,0:T(8,128)S(1)}, f32[8,5,128,128]{3,1,2,0:T(8,128)}, u32[]{:S(2)}) copy-start(f32[8,5,128,128]{3,1,2,0:T(8,128)} %copy.29) | copy-start | bytes 7864324
  125.6 4.1 %copy-start.4 = (bf16[8,1280,128]{2,1,0:T(8,128)(2,1)S(1)}, bf16[8,1280,128]{2,1,0:T(8,128)(2,1)}, u32[]{:S(2)}) copy-start(bf16[8,1280,128]{2,1,0:T(8,128)(2,1)} %copy-done.3) | copy-start | bytes 7864324
  125.6 4.1 %copy-start.13 = (bf16[8,5,128,128]{3,2,1,0:T(8,128)(2,1)S(1)}, bf16[8,5,128,128]{3,2,1,0:T(8,128)(2,1)}, u32[]{:S(2)}) copy-start(bf16[8,5,128,128]{3,2,1,0:T(8,128)(2,1)} %copy-done.12) | copy-start | bytes 3932164
  125.6 26.3 %collective-permute-start.7 = (f32[8,128,128]{2,1,0:T(8,128)S(1)}, f32[8,128,128]{2,1,0:T(8,128)S(1)}, u32[]{:S(2)}, u32[]{:S(2)}) collective-permute-start(f32[8,128,128]{2,1,0:T(8,128)S(1)} %multiply_add_fusion.1), channel_id=1, source_target_pairs={{8,0},{12,4},{9,1},{13,5},{10,2},{14,6},{11,3},{15,7},{24,16},{28,... | collective-permute-start | bytes 1572872 | tf_op jit(solution)/shard_map/ppermute | solution.py:17
  127.4 25.2 %slice-start.2 = ((s8[5242880]{0:T(1024)(128)(4,1)}), s8[4194304]{0:T(1024)(128)(4,1)S(1)}, s32[]{:S(2)}) async-start(s8[5242880]{0:T(1024)(128)(4,1)} %bitcast.113), calls=%async_computation.2 | async-start | bytes 8388608
  129.7 23.0 %slice-start.3 = ((s8[5242880]{0:T(1024)(128)(4,1)}), s8[1048576]{0:T(1024)(128)(4,1)S(1)}, s32[]{:S(2)}) async-start(s8[5242880]{0:T(1024)(128)(4,1)} %bitcast.113), calls=%async_computation.3 | async-start | bytes 2097152
  152.7 2.4 %copy-start.11 = (bf16[8,1280,128]{2,1,0:T(8,128)(2,1)S(1)}, bf16[8,1280,128]{2,1,0:T(8,128)(2,1)}, u32[]{:S(2)}) copy-start(bf16[8,1280,128]{2,1,0:T(8,128)(2,1)} %param.8) | copy-start | bytes 7864324
